TPU v7x, 256 devices: a whole 4x4x8 slice. The times are simulated.
256 devices in a mesh: dp: 32 (over z_hi, y, core), mp: 8 (over x, z_lo).
Axes of the slice: x: 4, y: 4, z: 8 (z_hi: 4, z_lo: 2; z = z_hi * 2 + z_lo), core: 2. Of those that a mesh axis runs over, the one named last changes fastest.
Arguments:
- activations: bfloat16 [2, 64, 384, 14336], P(None, 'dp', None, 'mp'), may hold values from -6 to 6
- out_grads: bfloat16 [2, 64, 384, 4096], P(None, 'dp', None, 'mp'), may hold values from -6 to 6
- proj_in: bfloat16 [14336, 64], P('mp'), may hold values from -0.046875 to 0.046875
- proj_out: bfloat16 [4096, 64], P('mp'), may hold values from -0.09375 to 0.09375
- store: bfloat16 [2, 65536, 4096], P(None, ('dp', 'mp')), may hold values from -0.09375 to 0.09375
- ckpt_rate: float32 [2], replicated, may hold values from 0.5 to 2
- store_group: int32 [65536], P(('dp', 'mp')), may hold values from 0 to 15
Outputs:
- scores: float32 [64, 65536], P(None, ('dp', 'mp'))
- group_scores: float32 [64, 16], replicated
All inputs are finite; a program needn't handle non-finite values.
Results may differ from a plain program's by a relative error of at most 0.005.
Values may be sent and summed in bfloat16 or wider, within the bound.
No kernel may reach another device: no remote copies, remote signals or barrier semaphores. Data moves between devices by JAX's collectives and lax.ppermute only.
A program may use at most 64 MiB of HBM per device.

v0:
```python
import jax
import jax.numpy as jnp
from jax import lax
from jax.sharding import PartitionSpec as P

GROUPS = 16


def shards(activations, out_grads, proj_in, proj_out, store, ckpt_rate, store_group):
    rank = proj_in.shape[1]
    seq_len = activations.shape[2]
    ex_local = activations.shape[1]
    scale = 1.0 / jnp.sqrt(jnp.float32(seq_len))
    part_in = jnp.einsum("cesf,fr->cesr", activations, proj_in, preferred_element_type=jnp.float32)
    part_out = jnp.einsum("cesf,fr->cesr", out_grads, proj_out, preferred_element_type=jnp.float32)
    stacked = jnp.concatenate([part_in, part_out], axis=3)
    summed = lax.psum(stacked, "mp")
    low_in = summed[..., :rank].astype(jnp.bfloat16)
    low_grad = summed[..., rank:].astype(jnp.bfloat16)
    outer = jnp.einsum("cesa,cesb->ecab", low_in, low_grad, preferred_element_type=jnp.float32)
    query = (outer.reshape(ex_local, 2, rank * rank) * scale).astype(jnp.bfloat16)
    piece = lax.all_gather(query, "dp", axis=0, tiled=True)
    first = jnp.einsum("qk,rk->qr", piece[:, 0], store[0], preferred_element_type=jnp.float32)
    second = jnp.einsum("qk,rk->qr", piece[:, 1], store[1], preferred_element_type=jnp.float32)
    scores = ckpt_rate[0] * first + ckpt_rate[1] * second
    member = (store_group[:, None] == jnp.arange(GROUPS, dtype=jnp.int32)[None, :]).astype(
        jnp.float32
    )
    partial_totals = jnp.dot(scores, member, precision=lax.Precision.HIGHEST)
    totals = lax.psum(partial_totals, ("dp", "mp"))
    store_rows = store.shape[1] * lax.axis_size("dp") * lax.axis_size("mp")
    group_scores = totals / jnp.sqrt(jnp.float32(store_rows) / jnp.float32(GROUPS))
    return (scores, group_scores)


def solution(mesh):
    placed = (
        P(None, "dp", None, "mp"),
        P(None, "dp", None, "mp"),
        P("mp", None),
        P("mp", None),
        P(None, ("dp", "mp"), None),
        P(),
        P(("dp", "mp")),
    )
    return jax.shard_map(
        shards, mesh=mesh, in_specs=placed, out_specs=(P(None, ("dp", "mp")), P()), check_vma=False
    )
```

profile of v0, /device:TPU:1, one launch (start us, length us, event | category | flops | bytes accessed | tf_op | source)
XLA Modules:
  0.0 203.9 jit_solution(9762679956642732704)
XLA Ops:
  7.2 0.0 copy-start
  7.2 0.0 copy-start.1
  7.2 0.0 all-gather.2.cloned.1.call-start
  7.2 4.4 %fusion.16 = f32[2,2,384,64]{2,3,1,0:T(8,128)S(1)} fusion(bf16[2,2,384,1792]{3,2,1,0:T(8,128)(2,1)} %param.7, bf16[1792,64]{0,1:T(8,128)(2,1)} %param.9), kind=kOutput, calls=%fused_computation.14 | convolution fusion | flops 352321536 | bytes 6127616 | tf_op jit(solution)/shard_map/cesf,fr->cesr/dot_general | solution.py:14
  11.7 0.0 copy-done
  11.7 0.0 copy-done.1
  11.7 0.0 copy-start.3
  11.7 0.6 fusion.21
  12.3 0.1 pad_maximum_fusion
  12.4 43.3 %all-reduce.1 = bf16[2,2,384,128]{2,3,1,0:T(8,128)(2,1)S(1)} all-reduce(f32[2,2,384,128]{2,3,1,0:T(8,128)S(1)} %pad_maximum_fusion), channel_id=1, replica_groups=mesh['dp'=32,'mp'=8] {'mp'}, use_global_device_ids=true, to_apply=%region_0.0 | all-reduce | flops 196608 | bytes 1179648 | tf_op jit(solution)/shard_map/psum | solution.py:17
  55.7 0.2 fusion.6
  55.9 0.7 convert_element_type.10
  56.7 0.0 all-gather.2.cloned.1.call-update
  56.7 0.0 copy-done.3
  56.7 0.6 fusion.26
  57.3 0.0 copy-start.4
  57.3 57.2 %all-gather.2.cloned.1.call-done = bf16[64,2,4096]{2,1,0:T(2,128)(2,1)} async-done(((bf16[2,2,4096]{2,1,0:T(2,128)(2,1)}), bf16[64,2,4096]{2,1,0:T(2,128)(2,1)}) %all-gather.2.cloned.1.call-update) | async-done | bytes 1048592 | tf_op jit(solution)/shard_map/all_gather | solution.py:22
  114.6 0.0 copy-start.5
  114.6 3.7 %fusion.24 = (bf16[64,1,4096]{2,1,0:T(2,128)(2,1)S(1)}, bf16[64,1,4096]{2,1,0:T(2,128)(2,1)S(1)}) fusion(bf16[64,2,4096]{2,1,0:T(2,128)(2,1)} %all-gather.2.cloned.1.call-done), kind=kLoop, calls=%fused_computation.24 | loop fusion | bytes 2097152 | tf_op jit(solution)/shard_map/slice | solution.py:23
  118.3 0.0 copy-done.5
  118.3 1.6 fusion.13
  119.9 1.6 fusion.10
  121.4 0.0 copy-done.4
  121.5 0.0 copy-start.2
  121.5 0.3 fusion.20
  121.8 74.6 %psum.15 = f32[64,16]{0,1:T(8,128)S(1)} all-reduce(f32[64,16]{0,1:T(8,128)S(1)} %fusion.20), channel_id=1, replica_groups=mesh['dp'=32,'mp'=8] {'dp','mp'}, use_global_device_ids=true, to_apply=%region_1.0 | all-reduce | flops 1024 | bytes 8192 | tf_op jit(solution)/shard_map/psum | solution.py:30
  196.4 0.6 broadcast_multiply_fusion
  197.0 0.0 copy-done.2
  (1 shorter events, 0.0 us)
Async XLA Ops:
  7.2 4.5 %copy-start = (bf16[2,2,384,512]{3,2,1,0:T(8,128)(2,1)S(1)}, bf16[2,2,384,512]{3,2,1,0:T(8,128)(2,1)}, u32[]{:S(2)}) copy-start(bf16[2,2,384,512]{3,2,1,0:T(8,128)(2,1)} %param.8) | copy-start | bytes 4718596
  7.2 4.5 %copy-start.1 = (bf16[512,64]{0,1:T(8,128)(2,1)S(1)}, bf16[512,64]{0,1:T(8,128)(2,1)}, u32[]{:S(2)}) copy-start(bf16[512,64]{0,1:T(8,128)(2,1)} %param.10) | copy-start | bytes 196612
  7.2 107.4 %all-gather.2.cloned.1.call-start = ((), (), s32[]{:S(2)}) async-start(), calls=%async_computation | async-start | bytes 1081344 | tf_op jit(solution)/shard_map/all_gather | solution.py:22
  11.7 45.0 %copy-start.3 = (f32[2]{0:T(128)S(1)}, f32[2]{0:T(128)}, u32[]{:S(2)}) copy-start(f32[2]{0:T(128)} %param.12) | copy-start | bytes 28
  57.3 64.1 %copy-start.4 = (s32[256]{0:T(256)S(1)}, s32[256]{0:T(256)}, u32[]{:S(2)}) copy-start(s32[256]{0:T(256)} %param.13) | copy-start | bytes 3076
  114.6 3.7 %copy-start.5 = (bf16[2,256,4096]{2,1,0:T(8,128)(2,1)S(1)}, bf16[2,256,4096]{2,1,0:T(8,128)(2,1)}, u32[]{:S(2)}) copy-start(bf16[2,256,4096]{2,1,0:T(8,128)(2,1)} %param.11) | copy-start | bytes 12582916
  121.5 75.6 %copy-start.2 = (f32[64,256]{1,0:T(8,128)}, f32[64,256]{1,0:T(8,128)S(1)}, u32[]{:S(2)}) copy-start(f32[64,256]{1,0:T(8,128)S(1)} %fusion.10) | copy-start | bytes 196612
Sparse Core Ops, SparseCore 0:
  56.8 57.6 all-gather.1
where the time goes:
time: 204 us
  blocking collectives  118 us (58%)
  waiting for transfers between devices  57.3 us (28%)
  between operations  14.2 us (7%)
  matrix products  8.67 us (4%)
  local copies, waits for them, and re-layouts  5.12 us (3%)
    psum x1, blocking collectives, shards(): totals = lax.psum(partial_totals, ('dp', 'mp'))  74.6 us
    all_gather x1, waiting for transfers between devices, shards(): piece = lax.all_gather(query, 'dp', axis=0, tiled=True)  57.2 us
    psum x1, blocking collectives, shards(): summed = lax.psum(stacked, 'mp')  43.3 us
    dot_general x1, matrix products, shards(): jnp.einsum('cesf,fr->cesr', activations, proj_in, preferred_element_type=...  4.43 us
  transfers between devices with their start and end apart: 1, of which 1 were waited for; matrix products, arithmetic and copies ran while one was open for 0% of the time, Pallas kernels for 0%

commit v1 on v0

--- a/solution.py
+++ b/solution.py
@@ -19,7 +19,9 @@
     low_grad = summed[..., rank:].astype(jnp.bfloat16)
     outer = jnp.einsum("cesa,cesb->ecab", low_in, low_grad, preferred_element_type=jnp.float32)
     query = (outer.reshape(ex_local, 2, rank * rank) * scale).astype(jnp.bfloat16)
-    piece = lax.all_gather(query, "dp", axis=0, tiled=True)
+    piece = jnp.concatenate(
+        lax.all_to_all(jnp.stack([query] * lax.axis_size("dp")), "dp", 0, 0), axis=0
+    )
     first = jnp.einsum("qk,rk->qr", piece[:, 0], store[0], preferred_element_type=jnp.float32)
     second = jnp.einsum("qk,rk->qr", piece[:, 1], store[1], preferred_element_type=jnp.float32)
     scores = ckpt_rate[0] * first + ckpt_rate[1] * second

time: 204 us -> 180 us (0.88)
  waiting for transfers between devices: 57.3 us -> 28 us
  starting transfers between devices: 0.04 us -> 15.8 us
  between operations: 14.2 us -> 0.76 us
  matrix products: 8.67 us -> 11.6 us
    all_gather x1 -> x0, waiting for transfers between devices: 57.2 us -> none  [shards(): piece = lax.all_gather(query, 'dp', axis=0, tiled=True)]
    all_to_all x0 -> x1, waiting for transfers between devices: none -> 28 us  [shards(): lax.all_to_all(jnp.stack([query] * lax.axis_size('dp')), 'dp', 0, 0)]
    all_to_all x0 -> x1, starting transfers between devices: none -> 15.8 us  [shards(): lax.all_to_all(jnp.stack([query] * lax.axis_size('dp')), 'dp', 0, 0)]
    slice x1 -> x0, local copies, waits for them, and re-layouts: 3.7 us -> none  [shards(): piece[:, 0]]
where the time goes in v1:
time: 180 us
  blocking collectives  117 us (65%)
  waiting for transfers between devices  28 us (16%)
  starting transfers between devices  15.8 us (9%)
  matrix products  11.6 us (6%)
  local copies, waits for them, and re-layouts  6.15 us (3%)
    psum x1, blocking collectives, shards(): totals = lax.psum(partial_totals, ('dp', 'mp'))  73.6 us
    psum x1, blocking collectives, shards(): summed = lax.psum(stacked, 'mp')  43.3 us
    all_to_all x1, waiting for transfers between devices, shards(): lax.all_to_all(jnp.stack([query] * lax.axis_size('dp')), 'dp', 0, 0)  28 us
    all_to_all x1, starting transfers between devices, shards(): lax.all_to_all(jnp.stack([query] * lax.axis_size('dp')), 'dp', 0, 0)  15.8 us
    dot_general x1, matrix products, shards(): jnp.einsum('cesf,fr->cesr', activations, proj_in, preferred_element_type=...  4.44 us
  transfers between devices with their start and end apart: 1, of which 1 were waited for; matrix products, arithmetic and copies ran while one was open for 0% of the time, Pallas kernels for 0%

profile of v1, /device:TPU:1, one launch (start us, length us, event | category | flops | bytes accessed | tf_op | source)
XLA Modules:
  0.0 179.8 jit_solution(1642637515930545417)
XLA Ops:
  0.6 0.0 copy-start
  0.6 0.0 copy-start.1
  0.7 4.4 %fusion.16 = f32[2,2,384,64]{2,3,1,0:T(8,128)S(1)} fusion(bf16[2,2,384,1792]{3,2,1,0:T(8,128)(2,1)} %param.7, bf16[1792,64]{0,1:T(8,128)(2,1)} %param.9), kind=kOutput, calls=%fused_computation.14 | convolution fusion | flops 352321536 | bytes 6127616 | tf_op jit(solution)/shard_map/cesf,fr->cesr/dot_general | solution.py:14
  5.1 0.0 copy-done
  5.1 0.0 copy-done.1
  5.1 0.6 fusion.21
  5.7 0.0 copy-start.3
  5.7 0.1 pad_maximum_fusion
  5.8 43.3 %all-reduce.1 = bf16[2,2,384,128]{2,3,1,0:T(8,128)(2,1)S(1)} all-reduce(f32[2,2,384,128]{2,3,1,0:T(8,128)S(1)} %pad_maximum_fusion), channel_id=1, replica_groups=mesh['dp'=32,'mp'=8] {'mp'}, use_global_device_ids=true, to_apply=%region_0.0 | all-reduce | flops 196608 | bytes 1179648 | tf_op jit(solution)/shard_map/psum | solution.py:17
  49.2 0.2 fusion.6
  49.4 0.1 convert_element_type.12
  49.5 2.0 %stack.2 = bf16[32,2,2,4096]{3,1,2,0:T(2,128)(2,1)} broadcast(bf16[2,2,4096]{2,0,1:T(2,128)(2,1)S(1)} %copy.16), dimensions={1,2,3} | broadcast | bytes 1081344 | tf_op jit(solution)/shard_map/stack | solution.py:23
  51.5 15.8 %all-to-all-start = ((bf16[32,2,2,4096]{3,1,2,0:T(2,128)(2,1)}), bf16[32,2,2,4096]{3,1,2,0:T(2,128)(2,1)S(1)}, u32[]{:S(2)}, u32[]{:S(2)}) async-start(bf16[32,2,2,4096]{3,1,2,0:T(2,128)(2,1)} %stack.2), calls=%async_computation | async-start | bytes 2097152 | tf_op jit(solution)/shard_map/all_to_all | solution.py:23
  67.3 0.0 copy-done.3
  67.3 0.6 fusion.25
  67.9 28.0 %all-to-all-done = bf16[32,2,2,4096]{3,1,2,0:T(2,128)(2,1)S(1)} async-done(((bf16[32,2,2,4096]{3,1,2,0:T(2,128)(2,1)}), bf16[32,2,2,4096]{3,1,2,0:T(2,128)(2,1)S(1)}, u32[]{:S(2)}, u32[]{:S(2)}) %all-to-all-start) | async-done | bytes 1048608 | tf_op jit(solution)/shard_map/all_to_all | solution.py:23
  95.9 1.9 %copy.17 = bf16[32,2,2,4096]{3,1,0,2:T(2,128)(2,1)} copy(bf16[32,2,2,4096]{3,1,2,0:T(2,128)(2,1)S(1)} %all-to-all-done) | data formatting | bytes 2097152 | tf_op jit(solution)/shard_map/all_to_all | solution.py:23
  97.8 0.0 copy-start.4
  97.8 1.5 reshape.15
  99.3 3.0 %fusion.13 = f32[64,256]{1,0:T(8,128)S(1)} fusion(bf16[2,256,4096]{2,1,0:T(8,128)(2,1)} %param.11, bf16[64,2,4096]{2,0,1:T(8,128)(2,1)S(1)} %reshape.15, f32[]{:T(128)} %bitcast.7), kind=kOutput, calls=%fused_computation.10 | convolution fusion | flops 134234112 | bytes 2687488 | tf_op jit(solution)/shard_map/qk,rk->qr/dot_general | solution.py:26
  102.3 3.0 %fusion.10 = f32[64,256]{1,0:T(8,128)S(1)} fusion(f32[64,256]{1,0:T(8,128)S(1)} %fusion.13, bf16[2,256,4096]{2,1,0:T(8,128)(2,1)} %param.11, bf16[64,2,4096]{2,0,1:T(8,128)(2,1)S(1)} %reshape.15, f32[]{:T(128)} %bitcast), kind=kOutput, calls=%fused_computation.9 | convolution fusion | flops 134250496 | bytes 2753024 | tf_op jit(solution)/shard_map/qk,rk->qr/dot_general | solution.py:25
  105.3 0.0 copy-done.4
  105.3 0.0 copy-start.2
  105.3 0.3 fusion.20
  105.6 73.6 %psum.15 = f32[64,16]{0,1:T(8,128)S(1)} all-reduce(f32[64,16]{0,1:T(8,128)S(1)} %fusion.20), channel_id=1, replica_groups=mesh['dp'=32,'mp'=8] {'dp','mp'}, use_global_device_ids=true, to_apply=%region_1.0 | all-reduce | flops 1024 | bytes 8192 | tf_op jit(solution)/shard_map/psum | solution.py:32
  179.2 0.6 broadcast_multiply_fusion
  179.8 0.0 copy-done.2
  (2 shorter events, 0.1 us)
Async XLA Ops:
  0.6 4.5 %copy-start = (bf16[2,2,384,512]{3,2,1,0:T(8,128)(2,1)S(1)}, bf16[2,2,384,512]{3,2,1,0:T(8,128)(2,1)}, u32[]{:S(2)}) copy-start(bf16[2,2,384,512]{3,2,1,0:T(8,128)(2,1)} %param.8) | copy-start | bytes 4718596
  0.6 4.5 %copy-start.1 = (bf16[512,64]{0,1:T(8,128)(2,1)S(1)}, bf16[512,64]{0,1:T(8,128)(2,1)}, u32[]{:S(2)}) copy-start(bf16[512,64]{0,1:T(8,128)(2,1)} %param.10) | copy-start | bytes 196612
  5.7 61.6 %copy-start.3 = (f32[2]{0:T(128)S(1)}, f32[2]{0:T(128)}, u32[]{:S(2)}) copy-start(f32[2]{0:T(128)} %param.12) | copy-start | bytes 28
  51.5 44.4 %all-to-all-start = ((bf16[32,2,2,4096]{3,1,2,0:T(2,128)(2,1)}), bf16[32,2,2,4096]{3,1,2,0:T(2,128)(2,1)S(1)}, u32[]{:S(2)}, u32[]{:S(2)}) async-start(bf16[32,2,2,4096]{3,1,2,0:T(2,128)(2,1)} %stack.2), calls=%async_computation | async-start | bytes 2097152 | tf_op jit(solution)/shard_map/all_to_all | solution.py:23
  97.8 7.5 %copy-start.4 = (s32[256]{0:T(256)S(1)}, s32[256]{0:T(256)}, u32[]{:S(2)}) copy-start(s32[256]{0:T(256)} %param.13) | copy-start | bytes 3076
  105.3 74.5 %copy-start.2 = (f32[64,256]{1,0:T(8,128)}, f32[64,256]{1,0:T(8,128)S(1)}, u32[]{:S(2)}) copy-start(f32[64,256]{1,0:T(8,128)S(1)} %fusion.10) | copy-start | bytes 196612
